TPU v7x, 512 devices: a whole 4x4x16 slice. The times are simulated.
512 devices in a mesh: dp: 8 (over x, y_hi), expert: 64 (over y_lo, z, core).
Axes of the slice: x: 4, y: 4 (y_hi: 2, y_lo: 2; y = y_hi * 2 + y_lo), z: 16, core: 2. Of those that a mesh axis runs over, the one named last changes fastest.
Arguments:
- tokens: bfloat16 [65536, 2048], P(('dp', 'expert')), may hold values from -6 to 6
- out_grad: bfloat16 [65536, 2048], P(('dp', 'expert')), may hold values from -6 to 6
- combine: float32 [65536, 2], P(('dp', 'expert')), may hold values from 0.1 to 1
- expert_ids: int32 [65536, 2], P(('dp', 'expert')), may hold values from 0 to 63, all different within a row; in each aligned block of 128 rows (0 to 127, 128 to 255, ...) at most 5 rows name the same one
- gate_weight: bfloat16 [64, 2048, 768], P('expert', 'dp'), may hold values from -0.125 to 0.125
- up_weight: bfloat16 [64, 2048, 768], P('expert', 'dp'), may hold values from -0.125 to 0.125
- down_weight: bfloat16 [64, 2048, 768], P('expert', 'dp'), may hold values from -0.21875 to 0.21875
Outputs:
- token_grad: bfloat16 [65536, 2048], P(('dp', 'expert'))
- down_grad: bfloat16 [64, 2048, 768], P('expert', 'dp')
Inputs may be any that keep to these rules, and one draw needn't show every extreme that they name: `expert_ids`: each row names 2 different experts. Among the 128 rows of one device no expert is named more than 5 times, a bound that some block reaches.
All inputs are finite; a program needn't handle non-finite values.
Results may differ from a plain program's by a relative error of at most 0.012.
Values may be sent and summed in bfloat16 or wider, within the bound.
No kernel may reach another device: no remote copies, remote signals or barrier semaphores. Data moves between devices by JAX's collectives and lax.ppermute only.
A program may use at most 64 MiB of HBM per device.

v0:
```python
import jax
import jax.numpy as jnp
from jax import lax
from jax.sharding import PartitionSpec as P

TOP = 2


def forward_portion(rows_in, w_gate, w_up):
    gate_pre = jnp.dot(rows_in, w_gate, preferred_element_type=jnp.float32)
    up_pre = jnp.dot(rows_in, w_up, preferred_element_type=jnp.float32)
    sigmoid_gate = jax.nn.sigmoid(gate_pre)
    silu_gate = gate_pre * sigmoid_gate
    hidden = (silu_gate * up_pre).astype(jnp.bfloat16)
    return (gate_pre, up_pre, sigmoid_gate, silu_gate, hidden)


def body(tokens, out_grad, combine, expert_ids, gate_weight, up_weight, down_weight):
    token_rows = tokens.shape[0]
    embedding_width = tokens.shape[1]
    expert_count = lax.axis_size("expert")
    capacity = token_rows * TOP * 5 // (4 * expert_count)
    positions = expert_count * capacity
    flattened_identifiers = expert_ids.reshape(-1)
    onehot = (
        flattened_identifiers[:, None] == jnp.arange(expert_count, dtype=jnp.int32)[None, :]
    ).astype(jnp.int32)
    earlier = jnp.cumsum(onehot, axis=0) - onehot
    slot_index = jnp.sum(earlier * onehot, axis=1)
    target = flattened_identifiers * capacity + slot_index
    matches = target[None, :] == jnp.arange(positions, dtype=jnp.int32)[:, None]
    picker = jnp.sum(
        matches.reshape(positions, token_rows, TOP).astype(jnp.float32), axis=2
    ).astype(jnp.bfloat16)
    slot_weight = jnp.sum(
        jnp.where(matches, combine.reshape(-1)[None, :], jnp.float32(0.0)), axis=1
    )
    row_send = jnp.dot(picker, tokens, preferred_element_type=jnp.float32).astype(jnp.bfloat16)
    row_send = row_send.reshape(expert_count, capacity, embedding_width)
    picked_grad = jnp.dot(picker, out_grad, preferred_element_type=jnp.float32)
    grad_send = (slot_weight[:, None] * picked_grad).astype(jnp.bfloat16)
    grad_send = grad_send.reshape(expert_count, capacity, embedding_width)
    gathered = (
        lax.all_gather(gate_weight, "dp", axis=1, tiled=True),
        lax.all_gather(up_weight, "dp", axis=1, tiled=True),
        lax.all_gather(down_weight, "dp", axis=1, tiled=True),
    )
    w_gate = gathered[0][0]
    w_up = gathered[1][0]
    w_down = gathered[2][0]
    rows_in, grads_in = (
        lax.all_to_all(row_send, "expert", split_axis=0, concat_axis=0, tiled=True),
        lax.all_to_all(grad_send, "expert", split_axis=0, concat_axis=0, tiled=True),
    )
    rows_in = rows_in.reshape(positions, embedding_width)
    grads_in = grads_in.reshape(positions, embedding_width)
    gate_pre, up_pre, sigmoid_gate, silu_gate, hidden = forward_portion(rows_in, w_gate, w_up)
    hidden_grad = jnp.dot(grads_in, w_down, preferred_element_type=jnp.float32)
    gate_grad = (
        hidden_grad * up_pre * sigmoid_gate * (1.0 + gate_pre * (1.0 - sigmoid_gate))
    ).astype(jnp.bfloat16)
    up_grad = (hidden_grad * silu_gate).astype(jnp.bfloat16)
    contract_hidden = (((1,), (1,)), ((), ()))
    row_grad = (
        lax.dot_general(gate_grad, w_gate, contract_hidden, preferred_element_type=jnp.float32)
        + lax.dot_general(up_grad, w_up, contract_hidden, preferred_element_type=jnp.float32)
    ).astype(jnp.bfloat16)
    back_rows = lax.all_to_all(
        row_grad.reshape(expert_count, capacity, embedding_width),
        "expert",
        split_axis=0,
        concat_axis=0,
        tiled=True,
    )
    token_grad = lax.dot_general(
        picker,
        back_rows.reshape(positions, embedding_width),
        (((0,), (0,)), ((), ())),
        preferred_element_type=jnp.float32,
    ).astype(jnp.bfloat16)
    down_grad = lax.psum_scatter(
        lax.dot_general(
            grads_in, hidden, (((0,), (0,)), ((), ())), preferred_element_type=jnp.float32
        ).astype(jnp.bfloat16),
        "dp",
        scatter_dimension=0,
        tiled=True,
    )
    return (token_grad, down_grad[None])


def solution(mesh):
    placed = (
        P(("dp", "expert"), None),
        P(("dp", "expert"), None),
        P(("dp", "expert"), None),
        P(("dp", "expert"), None),
        P("expert", "dp", None),
        P("expert", "dp", None),
        P("expert", "dp", None),
    )
    return jax.shard_map(
        body,
        mesh=mesh,
        in_specs=placed,
        out_specs=(P(("dp", "expert"), None), P("expert", "dp", None)),
        check_vma=False,
    )
```

profile of v0, /device:TPU:33, one launch (start us, length us, event | category | flops | bytes accessed | tf_op | source)
XLA Modules:
  0.0 401.3 jit_solution(16385939312701261271)
XLA Ops:
  7.2 0.0 copy-start
  7.2 0.0 all-gather.8.cloned.1.call-start
  7.2 0.7 all-gather.8.cloned.1.call-update
  7.9 0.8 copy.23
  8.7 0.1 eq.49
  8.8 0.1 eq.45
  9.0 0.6 reduce-window.6
  9.6 0.2 slice_reduce_fusion
  9.8 0.1 fusion.23
  9.9 0.1 reduce_sum.30
  10.1 0.1 copy.26
  10.2 0.8 copy.27
  11.0 0.1 broadcast_in_dim.21
  11.1 0.7 multiply_add_fusion.1
  11.9 0.1 select_reduce_fusion
  12.0 0.0 copy-done
  12.0 0.5 fusion.16
  12.5 1.6 reshape.61
  14.1 0.0 copy-start.2
  14.1 17.2 %all-to-all-start = ((bf16[64,5,2048]{2,1,0:T(8,128)(2,1)}), bf16[64,5,2048]{2,1,0:T(8,128)(2,1)S(1)}, u32[]{:S(2)}, u32[]{:S(2)}) async-start(bf16[64,5,2048]{2,1,0:T(8,128)(2,1)} %reshape.61), calls=%async_computation | async-start | bytes 4194304 | tf_op jit(solution)/shard_map/all_to_all | solution.py:53
  31.4 0.0 all-gather.6.cloned.1.call-start
  31.4 0.7 all-gather.6.cloned.1.call-update
  32.1 0.0 copy-done.2
  32.1 1.6 convolution_convert_fusion.1
  33.7 3.4 reshape.63
  37.1 92.3 %all-to-all-done = bf16[64,5,2048]{2,1,0:T(8,128)(2,1)S(1)} async-done(((bf16[64,5,2048]{2,1,0:T(8,128)(2,1)}), bf16[64,5,2048]{2,1,0:T(8,128)(2,1)S(1)}, u32[]{:S(2)}, u32[]{:S(2)}) %all-to-all-start) | async-done | bytes 1310752 | tf_op jit(solution)/shard_map/all_to_all | solution.py:53
  129.4 7.1 %all-to-all-start.1 = ((bf16[64,5,2048]{2,1,0:T(8,128)(2,1)}), bf16[64,5,2048]{2,1,0:T(8,128)(2,1)}, u32[]{:S(2)}, u32[]{:S(2)}) async-start(bf16[64,5,2048]{2,1,0:T(8,128)(2,1)} %reshape.63), calls=%async_computation.1 | async-start | bytes 4194304 | tf_op jit(solution)/shard_map/all_to_all | solution.py:52
  136.6 0.0 all-gather.4.cloned.1.call-start
  136.6 0.7 all-gather.4.cloned.1.call-update
  137.3 0.2 reduce-scatter.2.cloned.1.call-start
  137.5 1.4 reshape.62
  139.0 95.6 %all-to-all-done.1 = bf16[64,5,2048]{2,1,0:T(8,128)(2,1)} async-done(((bf16[64,5,2048]{2,1,0:T(8,128)(2,1)}), bf16[64,5,2048]{2,1,0:T(8,128)(2,1)}, u32[]{:S(2)}, u32[]{:S(2)}) %all-to-all-start.1) | async-done | bytes 1310752 | tf_op jit(solution)/shard_map/all_to_all | solution.py:52
  234.5 2.6 reshape.64
  237.1 0.0 all-gather.8.cloned.1.call-done
  237.1 4.0 %fusion.2 = f32[320,768]{1,0:T(8,128)} fusion(bf16[320,2048]{1,0:T(8,128)(2,1)S(1)} %reshape.64, bf16[1,2048,768]{2,1,0:T(8,128)(2,1)} %all-gather.8.cloned.1.call-done), kind=kOutput, calls=%fused_computation.3 | convolution fusion | flops 1006632960 | bytes 5439488 | tf_op jit(solution)/shard_map/dot_general | solution.py:10
  241.2 0.0 copy-start.1
  241.2 0.0 all-gather.6.cloned.1.call-done
  241.2 0.0 copy-start.5
  241.2 3.2 fusion.6
  244.4 0.0 copy-start.7
  244.4 1.0 copy-done.7
  245.4 0.0 copy-done.1
  245.4 0.0 copy-done.5
  245.4 3.7 convolution_convert_fusion
  249.0 0.0 reduce-scatter.2.cloned.1.call-update
  249.1 0.0 copy-start.6
  249.1 20.1 %all-gather.4.cloned.1.call-done = bf16[1,2048,768]{2,1,0:T(8,128)(2,1)} async-done(((bf16[1,256,768]{2,1,0:T(8,128)(2,1)}), bf16[1,2048,768]{2,1,0:T(8,128)(2,1)}) %all-gather.4.cloned.1.call-update) | async-done | bytes 3145744 | tf_op jit(solution)/shard_map/all_gather | solution.py:46
  269.2 0.0 copy-start.3
  269.2 0.0 copy-start.8
  269.2 3.2 fusion.8
  272.4 0.0 copy-done.6
  272.5 0.0 copy-done.3
  272.5 0.0 copy-done.8
  272.5 0.0 copy-start.4
  272.5 1.3 fusion
  273.8 0.5 copy-done.4
  274.4 2.3 fusion.13
  276.7 2.4 reshape.65
  279.0 111.9 %all_to_all.15 = bf16[64,5,2048]{2,1,0:T(8,128)(2,1)} all-to-all(bf16[64,5,2048]{2,1,0:T(8,128)(2,1)S(1)} %reshape.65), channel_id=1, replica_groups=mesh['dp'=8,'expert'=64] {'expert'}, dimensions={0} | all-to-all | bytes 2621440 | tf_op jit(solution)/shard_map/all_to_all | solution.py:68
  391.0 2.6 reshape.66
  393.5 1.3 convolution_convert_fusion.2
  394.8 0.0 reduce-scatter.2.cloned.1.call-done
  (5 shorter events, 0.1 us)
Async XLA Ops:
  7.2 4.8 %copy-start = (bf16[128,2048]{1,0:T(8,128)(2,1)S(1)}, bf16[128,2048]{1,0:T(8,128)(2,1)}, u32[]{:S(2)}) copy-start(bf16[128,2048]{1,0:T(8,128)(2,1)} %param.8) | copy-start | bytes 1572868
  7.2 229.9 %all-gather.8.cloned.1.call-start = ((), (), s32[]{:S(2)}) async-start(), calls=%async_computation.6 | async-start | bytes 3538944 | tf_op jit(solution)/shard_map/all_gather | solution.py:44
  14.1 18.0 %copy-start.2 = (bf16[128,2048]{1,0:T(8,128)(2,1)S(1)}, bf16[128,2048]{1,0:T(8,128)(2,1)}, u32[]{:S(2)}) copy-start(bf16[128,2048]{1,0:T(8,128)(2,1)} %param.7) | copy-start | bytes 1572868
  14.1 115.3 %all-to-all-start = ((bf16[64,5,2048]{2,1,0:T(8,128)(2,1)}), bf16[64,5,2048]{2,1,0:T(8,128)(2,1)S(1)}, u32[]{:S(2)}, u32[]{:S(2)}) async-start(bf16[64,5,2048]{2,1,0:T(8,128)(2,1)} %reshape.61), calls=%async_computation | async-start | bytes 4194304 | tf_op jit(solution)/shard_map/all_to_all | solution.py:53
  31.4 209.8 %all-gather.6.cloned.1.call-start = ((), (), s32[]{:S(2)}) async-start(), calls=%async_computation.5 | async-start | bytes 3538944 | tf_op jit(solution)/shard_map/all_gather | solution.py:45
  129.4 105.1 %all-to-all-start.1 = ((bf16[64,5,2048]{2,1,0:T(8,128)(2,1)}), bf16[64,5,2048]{2,1,0:T(8,128)(2,1)}, u32[]{:S(2)}, u32[]{:S(2)}) async-start(bf16[64,5,2048]{2,1,0:T(8,128)(2,1)} %reshape.63), calls=%async_computation.1 | async-start | bytes 4194304 | tf_op jit(solution)/shard_map/all_to_all | solution.py:52
  136.6 132.7 %all-gather.4.cloned.1.call-start = ((), (), s32[]{:S(2)}) async-start(), calls=%async_computation.4 | async-start | bytes 3538944 | tf_op jit(solution)/shard_map/all_gather | solution.py:46
  137.3 257.5 %reduce-scatter.2.cloned.1.call-start = ((), (), s32[]{:S(2)}) async-start(), calls=%async_computation.7 | async-start | bytes 3538944 | tf_op jit(solution)/shard_map/reduce_scatter | solution.py:81
  241.2 4.2 %copy-start.1 = (bf16[320,2048]{1,0:T(8,128)(2,1)S(1)}, bf16[320,2048]{1,0:T(8,128)(2,1)}, u32[]{:S(2)}) copy-start(bf16[320,2048]{1,0:T(8,128)(2,1)} %reshape.62) | copy-start | bytes 3932164
  241.2 4.2 %copy-start.5 = (f32[320,768]{1,0:T(8,128)S(1)}, f32[320,768]{1,0:T(8,128)}, u32[]{:S(2)}) copy-start(f32[320,768]{1,0:T(8,128)} %fusion.2) | copy-start | bytes 2949124
  244.4 1.0 copy-start.7
  249.1 23.4 %copy-start.6 = (f32[320,768]{1,0:T(8,128)S(1)}, f32[320,768]{1,0:T(8,128)}, u32[]{:S(2)}) copy-start(f32[320,768]{1,0:T(8,128)} %fusion.2) | copy-start | bytes 2949124
  269.2 3.2 copy-start.3
  269.2 3.2 copy-start.8
  272.5 1.9 copy-start.4
Sparse Core Ops, SparseCore 0:
  11.2 88.6 all-gather.7
  103.0 82.7 all-gather.5
  189.0 80.1 all-gather.3
  274.4 99.4 reduce-scatter.1
where the time goes:
time: 402 us; the launch traced here: 401 us
  waiting for transfers between devices  210 us (52%)
  blocking collectives  112 us (28%)
  starting transfers between devices  24.7 us (6%)
  matrix products  21.1 us (5%)
  local copies, waits for them, and re-layouts  17.9 us (4%)
  between operations  14 us (3%)
    all_to_all x1, blocking collectives, body(): lax.all_to_all(row_grad.reshape(expert_count, capacity, embedding_width),...  112 us
    all_to_all x1, waiting for transfers between devices, body(): lax.all_to_all(row_send, 'expert', split_axis=0, concat_axis=0, tiled=True)  95.6 us
    all_to_all x1, waiting for transfers between devices, body(): lax.all_to_all(grad_send, 'expert', split_axis=0, concat_axis=0, tiled=True)  92.3 us
    all_gather x1, waiting for transfers between devices, body(): lax.all_gather(down_weight, 'dp', axis=1, tiled=True)  20.1 us
    all_to_all x1, starting transfers between devices, body(): lax.all_to_all(grad_send, 'expert', split_axis=0, concat_axis=0, tiled=True)  17.2 us
  transfers between devices with their start and end apart: 6, of which 3 were waited for; matrix products, arithmetic and copies ran while one was open for 10% of the time, Pallas kernels for 0%

commit v1 on v0

--- a/solution.py
+++ b/solution.py
@@ -43,7 +43,12 @@
     gathered = (
         lax.all_gather(gate_weight, "dp", axis=1, tiled=True),
         lax.all_gather(up_weight, "dp", axis=1, tiled=True),
-        lax.all_gather(down_weight, "dp", axis=1, tiled=True),
+        jnp.concatenate(
+            jax.lax.all_to_all(
+                jnp.stack([down_weight for _ in range(jax.lax.axis_size("dp"))]), "dp", 0, 0
+            ),
+            axis=1,
+        ),
     )
     w_gate = gathered[0][0]
     w_up = gathered[1][0]

time: 402 us -> 429 us (1.067)
  waiting for transfers between devices: 210 us -> 232 us
  starting transfers between devices: 24.7 us -> 30.9 us
  blocking collectives: 112 us -> 106 us
    all_to_all x0 -> x1, waiting for transfers between devices: none -> 40.8 us  [body(): jax.lax.all_to_all(jnp.stack([down_weight for _ in range(jax.lax.axis_siz...]
    all_gather x1 -> x0, waiting for transfers between devices: 20.1 us -> none  [body(): lax.all_gather(down_weight, 'dp', axis=1, tiled=True)]
    all_to_all x1, blocking collectives: 112 us -> 106 us  [body(): lax.all_to_all(row_grad.reshape(expert_count, capacity, embedding_width),...]
    all_to_all x0 -> x1, starting transfers between devices: none -> 6.36 us  [body(): jax.lax.all_to_all(jnp.stack([down_weight for _ in range(jax.lax.axis_siz...]
  transfers between devices with their start and end apart: 6 -> 6, of which waited for: 3 -> 3; matrix products, arithmetic and copies ran while one was open for 10% -> 7% of each run, Pallas kernels for 0% -> 0%
where the time goes in v1:
time: 429 us
  waiting for transfers between devices  232 us (54%)
  blocking collectives  106 us (25%)
  starting transfers between devices  30.9 us (7%)
  matrix products  24.1 us (6%)
  local copies, waits for them, and re-layouts  20.8 us (5%)
  between operations  13.9 us (3%)
    all_to_all x1, blocking collectives, body(): lax.all_to_all(row_grad.reshape(expert_count, capacity, embedding_width),...  106 us
    all_to_all x1, waiting for transfers between devices, body(): lax.all_to_all(row_send, 'expert', split_axis=0, concat_axis=0, tiled=True)  97.2 us
    all_to_all x1, waiting for transfers between devices, body(): lax.all_to_all(grad_send, 'expert', split_axis=0, concat_axis=0, tiled=True)  92.3 us
    all_to_all x1, waiting for transfers between devices, body(): jax.lax.all_to_all(jnp.stack([down_weight for _ in range(jax.lax.axis_siz...  40.8 us
    all_to_all x1, starting transfers between devices, body(): lax.all_to_all(grad_send, 'expert', split_axis=0, concat_axis=0, tiled=True)  17.2 us
  transfers between devices with their start and end apart: 6, of which 3 were waited for; matrix products, arithmetic and copies ran while one was open for 7% of the time, Pallas kernels for 0%

profile of v1, /device:TPU:33, one launch (start us, length us, event | category | flops | bytes accessed | tf_op | source)
XLA Modules:
  0.0 428.6 jit_solution(10852453414962049748)
XLA Ops:
  7.2 0.0 copy-start
  7.2 0.8 copy.23
  8.0 0.1 eq.49
  8.2 0.1 eq.45
  8.3 0.6 reduce-window.6
  8.9 0.2 slice_reduce_fusion
  9.2 0.1 fusion.21
  9.3 0.1 reduce_sum.30
  9.4 0.1 copy.26
  9.5 0.7 multiply_add_fusion.1
  10.2 0.8 copy.27
  11.0 0.1 broadcast_in_dim.21
  11.2 0.2 select_reduce_fusion
  11.3 0.0 copy-done
  11.3 0.5 fusion.14
  11.8 1.6 reshape.64
  13.5 0.0 copy-start.2
  13.5 17.2 %all-to-all-start = ((bf16[64,5,2048]{2,1,0:T(8,128)(2,1)}), bf16[64,5,2048]{2,1,0:T(8,128)(2,1)S(1)}, u32[]{:S(2)}, u32[]{:S(2)}) async-start(bf16[64,5,2048]{2,1,0:T(8,128)(2,1)} %reshape.64), calls=%async_computation | async-start | bytes 4194304 | tf_op jit(solution)/shard_map/all_to_all | solution.py:58
  30.7 0.0 all-gather.5.cloned.1.call-start
  30.7 0.7 all-gather.5.cloned.1.call-update
  31.4 0.0 copy-done.2
  31.4 1.6 convolution_convert_fusion.1
  33.1 3.4 reshape.66
  36.5 0.0 copy-start.3
  36.5 92.3 %all-to-all-done = bf16[64,5,2048]{2,1,0:T(8,128)(2,1)S(1)} async-done(((bf16[64,5,2048]{2,1,0:T(8,128)(2,1)}), bf16[64,5,2048]{2,1,0:T(8,128)(2,1)S(1)}, u32[]{:S(2)}, u32[]{:S(2)}) %all-to-all-start) | async-done | bytes 1310752 | tf_op jit(solution)/shard_map/all_to_all | solution.py:58
  128.7 7.1 %all-to-all-start.2 = ((bf16[64,5,2048]{2,1,0:T(8,128)(2,1)}), bf16[64,5,2048]{2,1,0:T(8,128)(2,1)}, u32[]{:S(2)}, u32[]{:S(2)}) async-start(bf16[64,5,2048]{2,1,0:T(8,128)(2,1)} %reshape.66), calls=%async_computation.2 | async-start | bytes 4194304 | tf_op jit(solution)/shard_map/all_to_all | solution.py:57
  135.8 0.0 all-gather.3.cloned.1.call-start
  135.9 0.7 all-gather.3.cloned.1.call-update
  136.6 97.2 %all-to-all-done.2 = bf16[64,5,2048]{2,1,0:T(8,128)(2,1)} async-done(((bf16[64,5,2048]{2,1,0:T(8,128)(2,1)}), bf16[64,5,2048]{2,1,0:T(8,128)(2,1)}, u32[]{:S(2)}, u32[]{:S(2)}) %all-to-all-start.2) | async-done | bytes 1310752 | tf_op jit(solution)/shard_map/all_to_all | solution.py:57
  233.8 0.0 copy-done.3
  233.8 1.8 stack.2
  235.6 6.4 %all-to-all-start.1 = ((bf16[8,1,256,768]{3,2,1,0:T(8,128)(2,1)}), bf16[8,1,256,768]{3,2,1,0:T(8,128)(2,1)}, u32[]{:S(2)}, u32[]{:S(2)}) async-start(bf16[8,1,256,768]{3,2,1,0:T(8,128)(2,1)} %stack.2), calls=%async_computation.1 | async-start | bytes 6291456 | tf_op jit(solution)/shard_map/all_to_all | solution.py:47
  242.0 0.2 reduce-scatter.2.cloned.1.call-start
  242.2 1.4 reshape.65
  243.7 0.0 copy-start.1
  243.7 2.7 reshape.67
  246.3 40.8 %all-to-all-done.1 = bf16[8,1,256,768]{3,2,1,0:T(8,128)(2,1)} async-done(((bf16[8,1,256,768]{3,2,1,0:T(8,128)(2,1)}), bf16[8,1,256,768]{3,2,1,0:T(8,128)(2,1)}, u32[]{:S(2)}, u32[]{:S(2)}) %all-to-all-start.1) | async-done | bytes 3145760 | tf_op jit(solution)/shard_map/all_to_all | solution.py:47
  287.1 0.0 copy-done.1
  287.1 4.0 fusion.29
  291.1 0.0 all-gather.5.cloned.1.call-done
  291.1 4.0 fusion.2
  295.1 0.0 all-gather.3.cloned.1.call-done
  295.2 0.0 copy-start.6
  295.2 3.1 fusion.6
  298.3 0.0 copy-start.8
  298.3 0.9 copy-done.8
  299.3 0.0 copy-done.6
  299.3 3.7 convolution_convert_fusion
  302.9 0.0 copy-start.5
  302.9 0.0 copy-start.7
  302.9 0.0 reduce-scatter.2.cloned.1.call-update
  302.9 1.2 copy-done.5
  304.1 0.3 copy-done.7
  304.4 0.0 copy-start.4
  304.4 3.6 fusion
  308.1 0.0 copy-done.4
  308.1 2.3 fusion.11
  310.4 2.4 reshape.68
  312.7 105.5 %all_to_all.20 = bf16[64,5,2048]{2,1,0:T(8,128)(2,1)} all-to-all(bf16[64,5,2048]{2,1,0:T(8,128)(2,1)S(1)} %reshape.68), channel_id=1, replica_groups=mesh['dp'=8,'expert'=64] {'expert'}, dimensions={0} | all-to-all | bytes 2621440 | tf_op jit(solution)/shard_map/all_to_all | solution.py:73
  418.2 2.6 reshape.69
  420.8 1.3 convolution_convert_fusion.2
  422.1 0.0 reduce-scatter.2.cloned.1.call-done
  (5 shorter events, 0.1 us)
Async XLA Ops:
  7.2 4.2 copy-start
  13.5 18.0 %copy-start.2 = (bf16[128,2048]{1,0:T(8,128)(2,1)S(1)}, bf16[128,2048]{1,0:T(8,128)(2,1)}, u32[]{:S(2)}) copy-start(bf16[128,2048]{1,0:T(8,128)(2,1)} %param.7) | copy-start | bytes 1572868
  13.5 115.3 %all-to-all-start = ((bf16[64,5,2048]{2,1,0:T(8,128)(2,1)}), bf16[64,5,2048]{2,1,0:T(8,128)(2,1)S(1)}, u32[]{:S(2)}, u32[]{:S(2)}) async-start(bf16[64,5,2048]{2,1,0:T(8,128)(2,1)} %reshape.64), calls=%async_computation | async-start | bytes 4194304 | tf_op jit(solution)/shard_map/all_to_all | solution.py:58
  30.7 260.5 %all-gather.5.cloned.1.call-start = ((), (), s32[]{:S(2)}) async-start(), calls=%async_computation.6 | async-start | bytes 3538944 | tf_op jit(solution)/shard_map/all_gather | solution.py:44
  36.5 197.3 %copy-start.3 = (bf16[1,256,768]{2,1,0:T(8,128)(2,1)S(1)}, bf16[1,256,768]{2,1,0:T(8,128)(2,1)}, u32[]{:S(2)}) copy-start(bf16[1,256,768]{2,1,0:T(8,128)(2,1)} %param.13) | copy-start | bytes 1179652
  128.7 105.1 %all-to-all-start.2 = ((bf16[64,5,2048]{2,1,0:T(8,128)(2,1)}), bf16[64,5,2048]{2,1,0:T(8,128)(2,1)}, u32[]{:S(2)}, u32[]{:S(2)}) async-start(bf16[64,5,2048]{2,1,0:T(8,128)(2,1)} %reshape.66), calls=%async_computation.2 | async-start | bytes 4194304 | tf_op jit(solution)/shard_map/all_to_all | solution.py:57
  135.8 159.3 %all-gather.3.cloned.1.call-start = ((), (), s32[]{:S(2)}) async-start(), calls=%async_computation.5 | async-start | bytes 3538944 | tf_op jit(solution)/shard_map/all_gather | solution.py:45
  235.6 51.5 %all-to-all-start.1 = ((bf16[8,1,256,768]{3,2,1,0:T(8,128)(2,1)}), bf16[8,1,256,768]{3,2,1,0:T(8,128)(2,1)}, u32[]{:S(2)}, u32[]{:S(2)}) async-start(bf16[8,1,256,768]{3,2,1,0:T(8,128)(2,1)} %stack.2), calls=%async_computation.1 | async-start | bytes 6291456 | tf_op jit(solution)/shard_map/all_to_all | solution.py:47
  242.0 180.1 %reduce-scatter.2.cloned.1.call-start = ((), (), s32[]{:S(2)}) async-start(), calls=%async_computation.7 | async-start | bytes 3538944 | tf_op jit(solution)/shard_map/reduce_scatter | solution.py:86
  243.7 43.5 %copy-start.1 = (bf16[320,2048]{1,0:T(8,128)(2,1)S(1)}, bf16[320,2048]{1,0:T(8,128)(2,1)}, u32[]{:S(2)}) copy-start(bf16[320,2048]{1,0:T(8,128)(2,1)} %reshape.65) | copy-start | bytes 3932164
  295.2 4.1 copy-start.6
  298.3 1.0 copy-start.8
  302.9 1.2 copy-start.5
  302.9 1.5 copy-start.7
  304.4 3.7 copy-start.4
Sparse Core Ops, SparseCore 0:
  34.7 86.0 all-gather.4
  139.8 85.7 all-gather.2
  303.1 92.4 reduce-scatter.1
